TPU v7x, 128 devices: a whole 4x4x4 slice. The times are simulated.
128 devices in a mesh: dp: 2 (over core), seq: 16 (over z, x), head: 4 (over y).
Axes of the slice: x: 4, y: 4, z: 4, core: 2. Of those that a mesh axis runs over, the one named last changes fastest.
Arguments:
- queries: bfloat16 [2, 10240, 2048], P('dp', ('seq', 'head')), may hold values from -45 to 45
- key_rows: bfloat16 [2, 10240, 2048], P('dp', ('seq', 'head')), may hold values from -6 to 6
- values: bfloat16 [2, 10240, 2048], P('dp', ('seq', 'head')), may hold values from -6 to 6
- rand_blocks: int32 [160, 16, 4], P('seq', 'head'), may hold values from 0 to 159, as said below
- out_weight: bfloat16 [2048, 2048], P('head'), may hold values from -0.125 to 0.125
- cotangent: bfloat16 [2, 10240, 2048], P('dp', ('seq', 'head')), may hold values from -6 to 6
Outputs:
- layer_out: bfloat16 [2, 10240, 2048], P('dp', ('seq', 'head'))
- grad_queries: bfloat16 [2, 10240, 2048], P('dp', ('seq', 'head'))
- grad_keys: bfloat16 [2, 10240, 2048], P('dp', ('seq', 'head'))
- grad_values: bfloat16 [2, 10240, 2048], P('dp', ('seq', 'head'))
- weight_grad: float32 [2048, 2048], P('head')
Inputs may be any that keep to these rules, and one draw needn't show every extreme that they name: `rand_blocks`: key block b lies in range b // 10 of seq. Over the 10 query blocks of one index of seq and the 4 heads of one index of head, at most 15 of the listed random blocks lie in any one range of seq; in every draw, for every index of head, some range of seq receives exactly 15 of them from every index of seq.
All inputs are finite; a program needn't handle non-finite values.
Results may differ from a plain program's by a relative error of at most 0.034.
Values may be sent and summed in bfloat16 or wider, within the bound.
No kernel may reach another device: no remote copies, remote signals or barrier semaphores. Data moves between devices by JAX's collectives and lax.ppermute only.
A program may use at most 192 MiB of HBM per device.

v0:
```python
import math
import jax
import jax.numpy as jnp
from jax import lax
from jax.sharding import PartitionSpec as P

HEAD_SIZE = 128
BLOCK_TOKENS = 64


def with_halo(block, sides, width):
    for axis, dim in sides:
        count = lax.axis_size(axis)
        forward = [(i, i + 1) for i in range(count - 1)]
        backward = [(target, source) for source, target in forward]
        low = lax.ppermute(
            lax.slice_in_dim(block, block.shape[dim] - width, None, axis=dim), axis, forward
        )
        high = lax.ppermute(lax.slice_in_dim(block, 0, width, axis=dim), axis, backward)
        block = jnp.concatenate([low, block, high], axis=dim)
    return block


def broadcast_first(block, axis):
    count = lax.axis_size(axis)
    index = lax.axis_index(axis)
    step = 1
    while step < count:
        pairs = [(i, i + step) for i in range(step) if i + step < count]
        got = lax.ppermute(block, axis, pairs)
        block = jnp.where(index >= step, got, block)
        step *= 2
    return block


def reduce_to_first(block, axis):
    count = lax.axis_size(axis)
    step = 1
    while step * 2 < count:
        step *= 2
    while step >= 1:
        pairs = [(i + step, i) for i in range(step) if i + step < count]
        block = block + lax.ppermute(block, axis, pairs)
        step //= 2
    return block


def per_device(queries, key_rows, values, rand_blocks, out_weight, cotangent):
    block_len = BLOCK_TOKENS
    head_dim = HEAD_SIZE
    seq_count = lax.axis_size("seq")
    seq_index = lax.axis_index("seq")
    q_heads, k_heads, v_heads = (
        lax.all_to_all(queries, "head", split_axis=2, concat_axis=1, tiled=True),
        lax.all_to_all(key_rows, "head", split_axis=2, concat_axis=1, tiled=True),
        lax.all_to_all(values, "head", split_axis=2, concat_axis=1, tiled=True),
    )
    q_rows = q_heads[0]
    shard_len = q_rows.shape[0]
    width_cols = q_rows.shape[1]
    head_count = width_cols // head_dim
    block_count = shard_len // block_len
    rand_count = rand_blocks.shape[2]
    key_value = jnp.concatenate([k_heads[0], v_heads[0]], axis=1)
    padded = with_halo(key_value, (("seq", 0),), block_len)
    first_block = broadcast_first(key_value[:block_len], "seq")
    requests = jnp.transpose(rand_blocks, (0, 2, 1)).reshape(-1)
    request_count = requests.shape[0]
    head_of = jnp.arange(request_count, dtype=jnp.int32) % head_count
    capacity = 3 * request_count // (2 * seq_count)
    owners = requests // block_count
    offsets = requests % block_count
    one_hot = (owners[:, None] == jnp.arange(seq_count, dtype=jnp.int32)[None, :]).astype(jnp.int32)
    position = jnp.sum(one_hot * (jnp.cumsum(one_hot, axis=0) - 1), axis=1)
    slot_of = owners * capacity + position
    asked_codes = (
        jnp.full((seq_count * capacity,), -1, jnp.int32)
        .at[slot_of]
        .set(offsets * head_count + head_of)
        .reshape(seq_count, capacity)
    )
    asked_here = lax.all_to_all(asked_codes, "seq", split_axis=0, concat_axis=0, tiled=True)
    slot_total = seq_count * capacity
    pair_count = block_count * head_count
    asked_flat = asked_here.reshape(slot_total)
    serve_hot = (asked_flat[:, None] == jnp.arange(pair_count, dtype=jnp.int32)[None, :]).astype(
        jnp.bfloat16
    )
    pick_hot = (slot_of[:, None] == jnp.arange(slot_total, dtype=jnp.int32)[None, :]).astype(
        jnp.bfloat16
    )
    kv_pairs = jnp.transpose(
        key_value.reshape(block_count, block_len, 2, head_count, head_dim), (0, 3, 1, 2, 4)
    ).reshape(pair_count, block_len * 2 * head_dim)
    served = jnp.dot(serve_hot, kv_pairs, preferred_element_type=jnp.float32).astype(jnp.bfloat16)
    served = served.reshape(seq_count, capacity, block_len, 2 * head_dim)
    received = lax.all_to_all(served, "seq", split_axis=0, concat_axis=0, tiled=True)
    far_pairs = jnp.dot(
        pick_hot, received.reshape(slot_total, -1), preferred_element_type=jnp.float32
    ).astype(jnp.bfloat16)
    pair_view = padded.reshape(block_count + 2, block_len, 2, head_count, head_dim)
    window_pairs = jnp.stack(
        [pair_view[:block_count], pair_view[1 : block_count + 1], pair_view[2:]], axis=1
    ).reshape(block_count, 3 * block_len, 2, head_count, head_dim)
    window_keys = window_pairs[:, :, 0]
    window_vals = window_pairs[:, :, 1]
    first_pairs = first_block.reshape(block_len, 2, head_count, head_dim)
    first_keys = first_pairs[:, 0]
    first_vals = first_pairs[:, 1]
    far_view = far_pairs.reshape(block_count, rand_count, head_count, block_len, 2 * head_dim)
    far_keys = far_view[..., :head_dim]
    far_vals = far_view[..., head_dim:]
    global_ids = seq_index * block_count + jnp.arange(block_count, dtype=jnp.int32)
    block_total = seq_count * block_count
    window_live = jnp.stack([global_ids > 0, global_ids >= 0, global_ids < block_total - 1], axis=1)
    window_mask = jnp.repeat(window_live, block_len, axis=1)[None, :, None, :]
    query_blocks = q_rows.reshape(block_count, block_len, head_count, head_dim)
    softmax_scale = 1.0 / math.sqrt(head_dim)
    score_window = (
        jnp.einsum("ibhd,ikhd->hibk", query_blocks, window_keys, preferred_element_type=jnp.float32)
        * softmax_scale
    )
    score_first = (
        jnp.einsum("ibhd,khd->hibk", query_blocks, first_keys, preferred_element_type=jnp.float32)
        * softmax_scale
    )
    score_far = (
        jnp.einsum("ibhd,irhtd->hibrt", query_blocks, far_keys, preferred_element_type=jnp.float32)
        * softmax_scale
    )
    max_window = jnp.max(jnp.where(window_mask, score_window, -jnp.inf), axis=-1, keepdims=True)
    max_first = jnp.max(score_first, axis=-1, keepdims=True)
    max_far = jnp.max(score_far, axis=(-2, -1))[..., None]
    row_max = jnp.maximum(jnp.maximum(max_window, max_first), max_far)
    weight_window = jnp.where(window_mask, jnp.exp(score_window - row_max), 0.0)
    weight_first = jnp.exp(score_first - row_max)
    weight_far = jnp.exp(score_far - row_max[..., None])
    totals = (
        jnp.sum(weight_window, axis=-1, keepdims=True)
        + jnp.sum(weight_first, axis=-1, keepdims=True)
        + jnp.sum(weight_far, axis=(-2, -1))[..., None]
    )
    mixed = jnp.einsum(
        "hibk,ikhd->ibhd",
        weight_window.astype(jnp.bfloat16),
        window_vals,
        preferred_element_type=jnp.float32,
    )
    mixed = mixed + jnp.einsum(
        "hibk,khd->ibhd",
        weight_first.astype(jnp.bfloat16),
        first_vals,
        preferred_element_type=jnp.float32,
    )
    mixed = mixed + jnp.einsum(
        "hibrt,irhtd->ibhd",
        weight_far.astype(jnp.bfloat16),
        far_vals,
        preferred_element_type=jnp.float32,
    )
    totals_rows = jnp.transpose(totals, (1, 2, 0, 3))
    attn = (mixed / totals_rows).astype(jnp.bfloat16)
    logsum = row_max + jnp.log(totals)
    attn_rows = attn.reshape(shard_len, width_cols)
    layer_out = lax.psum_scatter(
        jnp.dot(attn_rows, out_weight, preferred_element_type=jnp.float32),
        "head",
        scatter_dimension=0,
        tiled=True,
    ).astype(jnp.bfloat16)[None]
    piece_flat = lax.all_gather(cotangent, "head", axis=1, tiled=True)[0]
    grad_piece = jnp.dot(piece_flat, out_weight.T, preferred_element_type=jnp.float32).astype(
        jnp.bfloat16
    )
    weight_acc = jnp.dot(attn_rows.T, piece_flat, preferred_element_type=jnp.float32)
    token_total = lax.axis_size("dp") * seq_count * shard_len
    weight_grad = lax.psum(weight_acc, ("dp", "seq")) * (1.0 / math.sqrt(token_total))
    grad_blocks = grad_piece.reshape(block_count, block_len, head_count, head_dim)
    delta_rows = jnp.sum(grad_blocks.astype(jnp.float32) * attn.astype(jnp.float32), axis=-1)
    row_delta = jnp.transpose(delta_rows, (2, 0, 1))[..., None]
    prob_window = jnp.where(window_mask, jnp.exp(score_window - logsum), 0.0)
    prob_first = jnp.exp(score_first - logsum)
    prob_far = jnp.exp(score_far - logsum[..., None])
    dprob_window = jnp.einsum(
        "ibhd,ikhd->hibk", grad_blocks, window_vals, preferred_element_type=jnp.float32
    )
    dprob_first = jnp.einsum(
        "ibhd,khd->hibk", grad_blocks, first_vals, preferred_element_type=jnp.float32
    )
    dprob_far = jnp.einsum(
        "ibhd,irhtd->hibrt", grad_blocks, far_vals, preferred_element_type=jnp.float32
    )
    dscore_window = (prob_window * (dprob_window - row_delta)).astype(jnp.bfloat16)
    dscore_first = (prob_first * (dprob_first - row_delta)).astype(jnp.bfloat16)
    dscore_far = (prob_far * (dprob_far - row_delta[..., None])).astype(jnp.bfloat16)
    grad_q = jnp.einsum(
        "hibk,ikhd->ibhd", dscore_window, window_keys, preferred_element_type=jnp.float32
    )
    grad_q = grad_q + jnp.einsum(
        "hibk,khd->ibhd", dscore_first, first_keys, preferred_element_type=jnp.float32
    )
    grad_q = grad_q + jnp.einsum(
        "hibrt,irhtd->ibhd", dscore_far, far_keys, preferred_element_type=jnp.float32
    )
    grad_q = (grad_q * softmax_scale).astype(jnp.bfloat16)
    key_window = (
        jnp.einsum(
            "hibk,ibhd->ikhd", dscore_window, query_blocks, preferred_element_type=jnp.float32
        )
        * softmax_scale
    )
    value_window = jnp.einsum(
        "hibk,ibhd->ikhd",
        prob_window.astype(jnp.bfloat16),
        grad_blocks,
        preferred_element_type=jnp.float32,
    )
    key_first = (
        jnp.einsum("hibk,ibhd->khd", dscore_first, query_blocks, preferred_element_type=jnp.float32)
        * softmax_scale
    )
    value_first = jnp.einsum(
        "hibk,ibhd->khd",
        prob_first.astype(jnp.bfloat16),
        grad_blocks,
        preferred_element_type=jnp.float32,
    )
    key_far = (
        jnp.einsum(
            "hibrt,ibhd->irhtd", dscore_far, query_blocks, preferred_element_type=jnp.float32
        )
        * softmax_scale
    )
    value_far = jnp.einsum(
        "hibrt,ibhd->irhtd",
        prob_far.astype(jnp.bfloat16),
        grad_blocks,
        preferred_element_type=jnp.float32,
    )
    window_terms = jnp.stack(
        [
            key_window.reshape(block_count, 3, block_len, head_count, head_dim),
            value_window.reshape(block_count, 3, block_len, head_count, head_dim),
        ],
        axis=3,
    )
    grad_pad = jnp.zeros((block_count + 2, block_len, 2, head_count, head_dim), jnp.float32)
    grad_pad = (
        grad_pad.at[:block_count]
        .add(window_terms[:, 0])
        .at[1 : block_count + 1]
        .add(window_terms[:, 1])
        .at[2:]
        .add(window_terms[:, 2])
    )
    global_grad = reduce_to_first(
        jnp.stack([key_first, value_first], axis=1).reshape(block_len, 2 * width_cols), "seq"
    ).reshape(block_len, 2, head_count, head_dim)
    grad_pad = grad_pad.at[1].add(jnp.where(seq_index == 0, global_grad, 0.0))
    rims = jnp.concatenate([grad_pad[0], grad_pad[block_count + 1]], axis=0).reshape(
        2 * block_len, 2 * width_cols
    )
    rim_sums = with_halo(rims.astype(jnp.bfloat16), (("seq", 0),), block_len).astype(rims.dtype)
    core = grad_pad[1 : block_count + 1].reshape(shard_len, 2 * width_cols)
    core = (
        core.at[:block_len]
        .add(rim_sums[:block_len])
        .at[shard_len - block_len :]
        .add(rim_sums[3 * block_len :])
    )
    core = core.reshape(block_count, block_len, 2, head_count, head_dim)
    far_terms = (
        jnp.concatenate([key_far, value_far], axis=-1)
        .reshape(request_count, block_len * 2 * head_dim)
        .astype(jnp.bfloat16)
    )
    outgoing = jnp.dot(pick_hot.T, far_terms, preferred_element_type=jnp.float32).astype(
        jnp.bfloat16
    )
    outgoing = outgoing.reshape(seq_count, capacity, block_len, 2 * head_dim)
    incoming = lax.all_to_all(outgoing, "seq", split_axis=0, concat_axis=0, tiled=True)
    added = jnp.dot(
        serve_hot.T, incoming.reshape(slot_total, -1), preferred_element_type=jnp.float32
    ).reshape(block_count, head_count, block_len, 2, head_dim)
    core = core + jnp.transpose(added, (0, 2, 3, 1, 4))
    grad_k = core[:, :, 0].reshape(shard_len, width_cols).astype(jnp.bfloat16)
    grad_v = core[:, :, 1].reshape(shard_len, width_cols).astype(jnp.bfloat16)
    grad_q_rows = grad_q.reshape(shard_len, width_cols)
    grad_queries, grad_keys, grad_values = (
        lax.all_to_all(grad_q_rows[None], "head", split_axis=1, concat_axis=2, tiled=True),
        lax.all_to_all(grad_k[None], "head", split_axis=1, concat_axis=2, tiled=True),
        lax.all_to_all(grad_v[None], "head", split_axis=1, concat_axis=2, tiled=True),
    )
    return (layer_out, grad_queries, grad_keys, grad_values, weight_grad)


def solution(mesh):
    in_specs = (
        P("dp", ("seq", "head"), None),
        P("dp", ("seq", "head"), None),
        P("dp", ("seq", "head"), None),
        P("seq", "head", None),
        P("head", None),
        P("dp", ("seq", "head"), None),
    )
    out_specs = (
        P("dp", ("seq", "head"), None),
        P("dp", ("seq", "head"), None),
        P("dp", ("seq", "head"), None),
        P("dp", ("seq", "head"), None),
        P("head", None),
    )
    return jax.shard_map(
        per_device, mesh=mesh, in_specs=in_specs, out_specs=out_specs, check_vma=False
    )
```

profile of v0, /device:TPU:0, one launch (start us, length us, event | category | flops | bytes accessed | tf_op | source)
XLA Modules:
  0.0 644.7 jit_solution(16865927430126323125)
XLA Ops:
  7.2 6.0 copy.227
  13.7 12.7 %reduce.20 = bf16[2048,160]{1,0:T(8,128)(2,1)S(1)} reduce(bf16[2048,1,160]{2,1,0:T(2,128)(2,1)} %bitcast.285, bf16[]{:T(256)} %broadcast.366), dimensions={1}, to_apply=%bitcast.240.reduce_sub_computation | reduce | bytes 1310722
  28.7 4.6 all-to-all-start
  34.1 5.9 copy.230
  39.9 12.6 %reduce.21 = bf16[2048,160]{1,0:T(8,128)(2,1)S(1)} reduce(bf16[2048,1,160]{2,1,0:T(2,128)(2,1)} %bitcast.289, bf16[]{:T(256)} %broadcast.366), dimensions={1}, to_apply=%bitcast.238.reduce_sub_computation | reduce | bytes 1310722
  55.0 4.8 all-to-all-start.1
  61.1 4.2 reshape.596
  65.3 4.5 copy.228
  70.4 4.4 reshape.594
  74.8 5.7 copy.231
  83.6 3.4 collective-permute-start
  90.1 9.4 %all-to-all-start.3 = ((s32[16,1,15]{2,1,0:T(1,128)}), s32[16,1,15]{2,1,0:T(1,128)S(1)}, u32[]{:S(2)}, u32[]{:S(2)}) async-start(s32[16,1,15]{2,1,0:T(1,128)} %bitcast.19), calls=%async_computation.3 | async-start | bytes 16384 | tf_op jit(solution)/shard_map/all_to_all | solution.py:82
  99.5 5.9 copy.235
  105.4 12.6 %reduce.19 = bf16[2048,160]{1,0:T(8,128)(2,1)S(1)} reduce(bf16[2048,1,160]{2,1,0:T(2,128)(2,1)} %bitcast.290, bf16[]{:T(256)} %broadcast.366), dimensions={1}, to_apply=%bitcast.242.reduce_sub_computation | reduce | bytes 1310722
  120.4 4.8 all-to-all-start.2
  127.1 4.6 pad_maximum_fusion.5
  133.5 3.8 copy.482
  137.3 4.3 reshape.545
  141.6 6.7 %convolution_convert_fusion.1 = bf16[240,16384]{1,0:T(8,128)(2,1)} fusion(bf16[40,16384]{1,0:T(8,128)(2,1)} %reshape.545, s32[240]{0:T(256)S(1)} %eq.85), kind=kOutput, calls=%fused_computation.2 | convolution fusion | flops 318514560 | bytes 9176000 | tf_op jit(solution)/shard_map/dot_general | solution.py:95
  148.2 8.7 %copy.340 = bf16[30,8,64,256]{3,2,1,0:T(8,128)(2,1)} copy(bf16[30,8,64,256]{3,1,2,0:T(8,128)(2,1)} %bitcast.266) | data formatting | bytes 15728640
  156.9 7.3 %all-to-all-start.4 = ((bf16[16,15,64,256]{3,2,1,0:T(8,128)(2,1)}), bf16[16,15,64,256]{3,2,1,0:T(8,128)(2,1)}, u32[]{:S(2)}, u32[]{:S(2)}) async-start(bf16[16,15,64,256]{3,2,1,0:T(8,128)(2,1)} %bitcast.269), calls=%async_computation.4 | async-start | bytes 15728640 | tf_op jit(solution)/shard_map/all_to_all | solution.py:97
  165.7 4.4 collective-permute-start.2
  170.8 4.2 reshape.598
  175.1 5.7 copy.236
  180.8 2.7 all_to_all.91
  189.7 78.3 %collective-permute-done.2 = bf16[64,1024]{1,0:T(8,128)(2,1)} collective-permute-done((bf16[64,1024]{1,0:T(8,128)(2,1)S(1)}, bf16[64,1024]{1,0:T(8,128)(2,1)}, u32[]{:S(2)}, u32[]{:S(2)}) %collective-permute-start.2) | collective-permute-done | bytes 131104 | tf_op jit(solution)/shard_map/ppermute | solution.py:30
  270.0 3.8 stack.30
  275.6 4.9 pad_maximum_fusion.1
  287.8 2.9 select_reduce_fusion
  293.3 4.1 fusion.75
  299.3 14.4 %copy.341 = bf16[30,8,64,256]{3,1,2,0:T(8,128)(2,1)} copy(bf16[30,8,64,256]{3,2,1,0:T(8,128)(2,1)} %bitcast.108) | data formatting | bytes 15728640
  313.7 4.8 convolution_convert_fusion.2
  338.3 3.9 fusion.22
  342.7 5.0 multiply_convert_fusion.1
  347.7 2.4 fusion.9
  354.3 3.8 fusion.94
  358.2 3.9 pad_maximum_fusion
  362.9 3.7 copy.344
  366.6 5.6 convolution_convert_fusion
  372.2 8.9 %copy.345 = bf16[30,8,64,256]{3,2,1,0:T(8,128)(2,1)} copy(bf16[30,8,64,256]{3,1,2,0:T(8,128)(2,1)} %bitcast.265) | data formatting | bytes 15728640
  381.1 9.6 %all-to-all-start.6 = ((bf16[16,15,64,256]{3,2,1,0:T(8,128)(2,1)}), bf16[16,15,64,256]{3,2,1,0:T(8,128)(2,1)}, u32[]{:S(2)}, u32[]{:S(2)}) async-start(bf16[16,15,64,256]{3,2,1,0:T(8,128)(2,1)} %bitcast.268), calls=%async_computation.7 | async-start | bytes 15728640 | tf_op jit(solution)/shard_map/all_to_all | solution.py:281
  394.5 4.7 fusion.26
  401.8 3.3 copy_dynamic-update-slice_fusion.1
  405.1 4.0 copy_dynamic-update-slice_fusion
  411.1 60.6 %collective-permute-done.6 = f32[64,1024]{1,0:T(8,128)S(1)} collective-permute-done((f32[64,1024]{1,0:T(8,128)}, f32[64,1024]{1,0:T(8,128)S(1)}, u32[]{:S(2)}, u32[]{:S(2)}) %collective-permute-start.6) | collective-permute-done | bytes 262176 | tf_op jit(solution)/shard_map/ppermute | solution.py:43
  475.6 13.3 %collective-permute-done.7 = f32[64,1024]{1,0:T(8,128)S(1)} collective-permute-done((f32[64,1024]{1,0:T(8,128)S(1)}, f32[64,1024]{1,0:T(8,128)S(1)}, u32[]{:S(2)}, u32[]{:S(2)}) %collective-permute-start.7) | collective-permute-done | bytes 262176 | tf_op jit(solution)/shard_map/ppermute | solution.py:43
  492.4 13.0 %collective-permute-done.8 = f32[64,1024]{1,0:T(8,128)S(1)} collective-permute-done((f32[64,1024]{1,0:T(8,128)S(1)}, f32[64,1024]{1,0:T(8,128)S(1)}, u32[]{:S(2)}, u32[]{:S(2)}) %collective-permute-start.8) | collective-permute-done | bytes 262176 | tf_op jit(solution)/shard_map/ppermute | solution.py:43
  508.1 8.7 %collective-permute-done.9 = f32[64,1024]{1,0:T(8,128)S(1)} collective-permute-done((f32[64,1024]{1,0:T(8,128)S(1)}, f32[64,1024]{1,0:T(8,128)S(1)}, u32[]{:S(2)}, u32[]{:S(2)}) %collective-permute-start.9) | collective-permute-done | bytes 262176 | tf_op jit(solution)/shard_map/ppermute | solution.py:43
  518.9 2.6 convert.26
  524.6 5.2 collective-permute-start.10
  529.8 2.6 fusion.72
  533.3 4.6 reduce.22
  539.3 3.8 slice.295
  543.2 4.1 reshape.554
  550.7 4.2 reshape.556
  554.9 4.3 all-to-all-start.5
  559.2 14.5 %copy.346 = bf16[30,8,64,256]{3,1,2,0:T(8,128)(2,1)} copy(bf16[30,8,64,256]{3,2,1,0:T(8,128)(2,1)} %bitcast.123) | data formatting | bytes 15728640
  573.7 13.9 %dot_general.103 = bf16[64,2,128,240]{2,1,0,3:T(2,128)(2,1)} reshape(bf16[16384,240]{0,1:T(8,128)(2,1)} %bitcast.270) | data formatting | bytes 15728640 | tf_op jit(solution)/shard_map/dot_general | solution.py:282
  587.6 10.2 %fusion.8 = bf16[10,64,2,4,128]{4,0,2,1,3:T(8,128)(2,1)S(1)} fusion(f32[10,64,2,4,128]{4,3,2,1,0:T(4,128)} %reshape.556, bf16[64,2,128,240]{2,1,0,3:T(2,128)(2,1)} %dot_general.103, s32[10,4]{0,1:T(4,128)S(1)} %multiply_add_fusion, s32[240]{0:T(256)S(1)} %eq.85), kind=kOutput, calls=%fused_computation.19 | convolution fusion | flops 315893120 | bytes 11797600 | tf_op jit(solution)/shard_map/dot_general | solution.py:282
  599.0 4.6 reduce.24
  605.0 4.9 all-to-all-start.8
  614.2 4.6 reduce.23
  620.1 4.8 all-to-all-start.7
  624.9 5.0 broadcast_multiply_fusion
  (224 shorter events, 114.0 us)
Async XLA Ops:
  7.2 286.1 %copy-start = (bf16[512,2048]{1,0:T(8,128)(2,1)S(1)}, bf16[512,2048]{1,0:T(8,128)(2,1)}, u32[]{:S(2)}) copy-start(bf16[512,2048]{1,0:T(8,128)(2,1)} %param.22) | copy-start | bytes 6291460
  13.7 19.6 %copy-start.30 = (s32[10,4,4]{0,2,1:T(4,128)S(1)}, s32[10,4,4]{0,2,1:T(4,128)}, u32[]{:S(2)}) copy-start(s32[10,4,4]{0,2,1:T(4,128)} %param.21) | copy-start | bytes 1924
  28.7 26.2 %all-to-all-start = ((bf16[4,2,40960]{2,1,0:T(2,128)(2,1)}), bf16[4,2,40960]{2,1,0:T(2,128)(2,1)}, u32[]{:S(2)}, u32[]{:S(2)}) async-start(bf16[4,2,40960]{2,1,0:T(2,128)(2,1)} %reshape.595), calls=%async_computation | async-start | bytes 1310720 | tf_op jit(solution)/shard_map/all_to_all | solution.py:55
  54.9 10.4 %copy-start.31 = (s32[160]{0:T(256)}, s32[160]{0:T(256)S(1)}, u32[]{:S(2)}) copy-start(s32[160]{0:T(256)S(1)} %get-tuple-element.107) | copy-start | bytes 1924
  55.0 15.4 %all-to-all-start.1 = ((bf16[4,2,40960]{2,1,0:T(2,128)(2,1)}), bf16[4,2,40960]{2,1,0:T(2,128)(2,1)}, u32[]{:S(2)}, u32[]{:S(2)}) async-start(bf16[4,2,40960]{2,1,0:T(2,128)(2,1)} %reshape.593), calls=%async_computation.1 | async-start | bytes 1310720 | tf_op jit(solution)/shard_map/all_to_all | solution.py:56
  61.1 27.2 %copy-start.32 = (s32[160]{0:T(256)}, s32[160]{0:T(256)S(1)}, u32[]{:S(2)}) copy-start(s32[160]{0:T(256)S(1)} %fusion.135) | copy-start | bytes 1924
  70.4 12.4 %copy-start.18 = (bf16[1,4,160,512]{3,2,1,0:T(8,128)(2,1)}, bf16[1,4,160,512]{3,2,1,0:T(8,128)(2,1)S(1)}, u32[]{:S(2)}) copy-start(bf16[1,4,160,512]{3,2,1,0:T(8,128)(2,1)S(1)} %copy.229) | copy-start | bytes 1966084
  82.7 0.8 copy-start.19
  83.6 42.9 %collective-permute-start = (bf16[64,1024]{1,0:T(8,128)(2,1)S(1)}, bf16[64,1024]{1,0:T(8,128)(2,1)S(1)}, u32[]{:S(2)}, u32[]{:S(2)}) collective-permute-start(bf16[64,1024]{1,0:T(8,128)(2,1)S(1)} %get-tuple-element.96), channel_id=1, source_target_pairs={{0,4},{4,8},{8,12},{12,16},{16,20},{20,24},{24,28},{28,32},{32,36}... | collective-permute-start | bytes 393224 | tf_op jit(solution)/shard_map/ppermute | solution.py:16
  87.0 40.1 %collective-permute-start.1 = (bf16[64,1024]{1,0:T(8,128)(2,1)S(1)}, bf16[64,1024]{1,0:T(8,128)(2,1)}, u32[]{:S(2)}, u32[]{:S(2)}) collective-permute-start(bf16[64,1024]{1,0:T(8,128)(2,1)S(1)} %get-tuple-element.97), channel_id=1, source_target_pairs={{4,0},{8,4},{12,8},{16,12},{20,16},{24,20},{28,24},{32,28},{36,32}... | collective-permute-start | bytes 393224 | tf_op jit(solution)/shard_map/ppermute | solution.py:19
  90.1 30.3 %all-to-all-start.3 = ((s32[16,1,15]{2,1,0:T(1,128)}), s32[16,1,15]{2,1,0:T(1,128)S(1)}, u32[]{:S(2)}, u32[]{:S(2)}) async-start(s32[16,1,15]{2,1,0:T(1,128)} %bitcast.19), calls=%async_computation.3 | async-start | bytes 16384 | tf_op jit(solution)/shard_map/all_to_all | solution.py:82
  120.4 36.6 %all-to-all-start.2 = ((bf16[4,2,40960]{2,1,0:T(2,128)(2,1)}), bf16[4,2,40960]{2,1,0:T(2,128)(2,1)}, u32[]{:S(2)}, u32[]{:S(2)}) async-start(bf16[4,2,40960]{2,1,0:T(2,128)(2,1)} %reshape.597), calls=%async_computation.2 | async-start | bytes 1310720 | tf_op jit(solution)/shard_map/all_to_all | solution.py:54
  126.5 0.7 copy-start.29
  156.9 142.3 %all-to-all-start.4 = ((bf16[16,15,64,256]{3,2,1,0:T(8,128)(2,1)}), bf16[16,15,64,256]{3,2,1,0:T(8,128)(2,1)}, u32[]{:S(2)}, u32[]{:S(2)}) async-start(bf16[16,15,64,256]{3,2,1,0:T(8,128)(2,1)} %bitcast.269), calls=%async_computation.4 | async-start | bytes 15728640 | tf_op jit(solution)/shard_map/all_to_all | solution.py:97
  164.2 129.1 %all-gather.2.cloned.1.call-start = ((), (), s32[]{:S(2)}) async-start(), calls=%async_computation.11 | async-start | bytes 3276800 | tf_op jit(solution)/shard_map/all_gather | solution.py:171
  164.9 460.0 %all-reduce.4.cloned.1.call-start = ((), (), s32[]{:S(2)}) async-start(), calls=%async_computation.12 | async-start | bytes 8388608 | tf_op jit(solution)/shard_map/psum | solution.py:177
  165.7 102.3 %collective-permute-start.2 = (bf16[64,1024]{1,0:T(8,128)(2,1)S(1)}, bf16[64,1024]{1,0:T(8,128)(2,1)}, u32[]{:S(2)}, u32[]{:S(2)}) collective-permute-start(bf16[64,1024]{1,0:T(8,128)(2,1)S(1)} %get-tuple-element.97), channel_id=1, source_target_pairs={{0,4},{1,5},{2,6},{3,7},{64,68},{65,69},{66,70},{67,71}} | collective-permute-start | bytes 393224 | tf_op jit(solution)/shard_map/ppermute | solution.py:30
  189.7 84.1 %copy-start.20 = (bf16[640,1024]{1,0:T(8,128)(2,1)S(1)}, bf16[640,1024]{1,0:T(8,128)(2,1)}, u32[]{:S(2)}) copy-start(bf16[640,1024]{1,0:T(8,128)(2,1)} %get-tuple-element.94) | copy-start | bytes 3932164
  268.7 12.8 %collective-permute-start.3 = (bf16[64,1024]{1,0:T(8,128)(2,1)}, bf16[64,1024]{1,0:T(8,128)(2,1)S(1)}, u32[]{:S(2)}, u32[]{:S(2)}) collective-permute-start(bf16[64,1024]{1,0:T(8,128)(2,1)} %broadcast_select_fusion), channel_id=1, source_target_pairs={{0,8},{4,12},{1,9},{5,13},{2,10},{6,14},{3,11},{7,15},{64,72},{68,... | collective-permute-start | bytes 393224 | tf_op jit(solution)/shard_map/ppermute | solution.py:30
  281.5 6.2 copy-start.9
  282.7 3.8 collective-permute-start.4
  284.0 3.8 copy-start.10
  286.5 4.2 collective-permute-start.5
  321.9 1.5 copy-start.4
  321.9 10.2 %copy-start.6 = (bf16[10,4,4,64,128]{4,3,2,1,0:T(8,128)(2,1)}, bf16[10,4,4,64,128]{4,3,2,1,0:T(8,128)(2,1)S(1)}, u32[]{:S(2)}) copy-start(bf16[10,4,4,64,128]{4,3,2,1,0:T(8,128)(2,1)S(1)} %get-tuple-element.81) | copy-start | bytes 7864324
  321.9 3.6 copy-start.11
  323.4 7.2 %copy-start.2 = (f32[4,10,4,64,64]{4,3,2,1,0:T(8,128)}, f32[4,10,4,64,64]{4,3,2,1,0:T(8,128)S(1)}, u32[]{:S(2)}) copy-start(f32[4,10,4,64,64]{4,3,2,1,0:T(8,128)S(1)} %get-tuple-element.109) | copy-start | bytes 7864324
  323.4 3.5 copy-start.7
  330.6 1.1 copy-start.27
  332.1 1.5 copy-start.25
  334.9 3.4 copy-start.24
  337.4 0.8 copy-start.16
  342.2 293.3 %reduce-scatter.2.cloned.1.call-start = ((), (), s32[]{:S(2)}) async-start(), calls=%async_computation.10 | async-start | bytes 6553600 | tf_op jit(solution)/shard_map/reduce_scatter | solution.py:165
  347.6 2.7 copy-start.12
  347.7 3.6 copy-start.14
  352.1 2.2 copy-start.17
  381.1 9.6 %copy-start.8 = (f32[4,10,64,64]{2,3,1,0:T(8,128)S(1)}, f32[4,10,64,64]{2,3,1,0:T(8,128)}, u32[]{:S(2)}) copy-start(f32[4,10,64,64]{2,3,1,0:T(8,128)} %get-tuple-element.113) | copy-start | bytes 1966084
  381.1 9.6 %copy-start.28 = (bf16[64,1,4,128]{3,2,1,0:T(4,128)(2,1)S(1)}, bf16[64,1,4,128]{3,2,1,0:T(4,128)(2,1)}, u32[]{:S(2)}) copy-start(bf16[64,1,4,128]{3,2,1,0:T(4,128)(2,1)} %get-tuple-element.98) | copy-start | bytes 196612
  381.1 173.8 %all-to-all-start.6 = ((bf16[16,15,64,256]{3,2,1,0:T(8,128)(2,1)}), bf16[16,15,64,256]{3,2,1,0:T(8,128)(2,1)}, u32[]{:S(2)}, u32[]{:S(2)}) async-start(bf16[16,15,64,256]{3,2,1,0:T(8,128)(2,1)} %bitcast.268), calls=%async_computation.7 | async-start | bytes 15728640 | tf_op jit(solution)/shard_map/all_to_all | solution.py:281
  393.2 78.5 %collective-permute-start.6 = (f32[64,1024]{1,0:T(8,128)}, f32[64,1024]{1,0:T(8,128)S(1)}, u32[]{:S(2)}, u32[]{:S(2)}) collective-permute-start(f32[64,1024]{1,0:T(8,128)} %reshape.553), channel_id=1, source_target_pairs={{32,0},{36,4},{40,8},{44,12},{48,16},{52,20},{56,24},{60,28},{33,1... | collective-permute-start | bytes 786440 | tf_op jit(solution)/shard_map/ppermute | solution.py:43
  399.2 1.1 copy-start.22
  399.2 1.8 copy-start.21
  472.7 17.6 %copy-start.5 = (bf16[10,4,4,64,128]{4,3,2,1,0:T(8,128)(2,1)S(1)}, bf16[10,4,4,64,128]{4,3,2,1,0:T(8,128)(2,1)}, u32[]{:S(2)}) copy-start(bf16[10,4,4,64,128]{4,3,2,1,0:T(8,128)(2,1)} %copy-done.4) | copy-start | bytes 7864324
  472.7 17.6 %copy-start.13 = (bf16[4,10,64,4,64]{2,4,3,1,0:T(8,128)(2,1)S(1)}, bf16[4,10,64,4,64]{2,4,3,1,0:T(8,128)(2,1)}, u32[]{:S(2)}) copy-start(bf16[4,10,64,4,64]{2,4,3,1,0:T(8,128)(2,1)} %copy-done.12) | copy-start | bytes 3932164
  472.7 16.2 %collective-permute-start.7 = (f32[64,1024]{1,0:T(8,128)S(1)}, f32[64,1024]{1,0:T(8,128)S(1)}, u32[]{:S(2)}, u32[]{:S(2)}) collective-permute-start(f32[64,1024]{1,0:T(8,128)S(1)} %add.228), channel_id=1, source_target_pairs={{16,0},{20,4},{24,8},{28,12},{17,1},{21,5},{25,9},{29,13},{18,2},{... | collective-permute-start | bytes 786440 | tf_op jit(solution)/shard_map/ppermute | solution.py:43
  475.6 16.8 %copy-start.3 = (f32[12,64,2,4,128]{4,3,2,1,0:T(4,128)}, f32[12,64,2,4,128]{4,3,2,1,0:T(4,128)S(1)}, u32[]{:S(2)}) copy-start(f32[12,64,2,4,128]{4,3,2,1,0:T(4,128)S(1)} %fusion.11) | copy-start | bytes 9437188
  488.9 16.4 %collective-permute-start.8 = (f32[64,1024]{1,0:T(8,128)S(1)}, f32[64,1024]{1,0:T(8,128)S(1)}, u32[]{:S(2)}, u32[]{:S(2)}) collective-permute-start(f32[64,1024]{1,0:T(8,128)S(1)} %add.229), channel_id=1, source_target_pairs={{8,0},{12,4},{9,1},{13,5},{10,2},{14,6},{11,3},{15,7},{72,64},{76,... | collective-permute-start | bytes 786440 | tf_op jit(solution)/shard_map/ppermute | solution.py:43
  505.4 11.4 %collective-permute-start.9 = (f32[64,1024]{1,0:T(8,128)S(1)}, f32[64,1024]{1,0:T(8,128)S(1)}, u32[]{:S(2)}, u32[]{:S(2)}) collective-permute-start(f32[64,1024]{1,0:T(8,128)S(1)} %add.230), channel_id=1, source_target_pairs={{4,0},{5,1},{6,2},{7,3},{68,64},{69,65},{70,66},{71,67}} | collective-permute-start | bytes 786440 | tf_op jit(solution)/shard_map/ppermute | solution.py:43
  518.9 11.0 %copy-start.15 = (bf16[10,192,4,128]{3,1,0,2:T(8,128)(2,1)S(1)}, bf16[10,192,4,128]{3,1,0,2:T(8,128)(2,1)}, u32[]{:S(2)}) copy-start(bf16[10,192,4,128]{3,1,0,2:T(8,128)(2,1)} %get-tuple-element.83) | copy-start | bytes 5898244
  518.9 11.0 %copy-start.23 = (bf16[4,10,64,192]{3,2,1,0:T(8,128)(2,1)S(1)}, bf16[4,10,64,192]{3,2,1,0:T(8,128)(2,1)}, u32[]{:S(2)}) copy-start(bf16[4,10,64,192]{3,2,1,0:T(8,128)(2,1)} %copy-done.22) | copy-start | bytes 2949124
  523.3 24.0 %collective-permute-start.11 = (bf16[64,1024]{1,0:T(8,128)(2,1)S(1)}, bf16[64,1024]{1,0:T(8,128)(2,1)}, u32[]{:S(2)}, u32[]{:S(2)}) collective-permute-start(bf16[64,1024]{1,0:T(8,128)(2,1)S(1)} %concatenate.41), channel_id=1, source_target_pairs={{4,0},{8,4},{12,8},{16,12},{20,16},{24,20},{28,24},{32,28},{36,32}... | collective-permute-start | bytes 393224 | tf_op jit(solution)/shard_map/ppermute | solution.py:19
  524.6 22.7 %collective-permute-start.10 = (bf16[64,1024]{1,0:T(8,128)(2,1)S(1)}, bf16[64,1024]{1,0:T(8,128)(2,1)}, u32[]{:S(2)}, u32[]{:S(2)}) collective-permute-start(bf16[64,1024]{1,0:T(8,128)(2,1)S(1)} %concatenate.40), channel_id=1, source_target_pairs={{0,4},{4,8},{8,12},{12,16},{16,20},{20,24},{24,28},{28,32},{32,36}... | collective-permute-start | bytes 393224 | tf_op jit(solution)/shard_map/ppermute | solution.py:16
  539.3 3.8 copy-start.26
  554.9 50.1 %all-to-all-start.5 = ((bf16[4,2,40960]{2,1,0:T(2,128)(2,1)}), bf16[4,2,40960]{2,1,0:T(2,128)(2,1)}, u32[]{:S(2)}, u32[]{:S(2)}) async-start(bf16[4,2,40960]{2,1,0:T(2,128)(2,1)} %reshape.599), calls=%async_computation.6 | async-start | bytes 1310720 | tf_op jit(solution)/shard_map/all_to_all | solution.py:290
  605.0 15.2 %all-to-all-start.8 = ((bf16[4,2,40960]{2,1,0:T(2,128)(2,1)}), bf16[4,2,40960]{2,1,0:T(2,128)(2,1)}, u32[]{:S(2)}, u32[]{:S(2)}) async-start(bf16[4,2,40960]{2,1,0:T(2,128)(2,1)} %reshape.603), calls=%async_computation.9 | async-start | bytes 1310720 | tf_op jit(solution)/shard_map/all_to_all | solution.py:292
  620.1 13.6 %all-to-all-start.7 = ((bf16[4,2,40960]{2,1,0:T(2,128)(2,1)}), bf16[4,2,40960]{2,1,0:T(2,128)(2,1)S(1)}, u32[]{:S(2)}, u32[]{:S(2)}) async-start(bf16[4,2,40960]{2,1,0:T(2,128)(2,1)} %reshape.601), calls=%async_computation.8 | async-start | bytes 1310720 | tf_op jit(solution)/shard_map/all_to_all | solution.py:291
  634.4 3.3 copy-start.1
Sparse Core Ops, SparseCore 0:
  166.7 37.1 all-gather.1
  342.3 194.1 all-reduce.3
  538.9 61.0 reduce-scatter.1
where the time goes:
time: 657 us; the launch traced here: 645 us
  local copies, waits for them, and re-layouts  209 us (32%)
  waiting for transfers between devices  175 us (27%)
  other arithmetic  95.2 us (14%)
  starting transfers between devices  80.8 us (12%)
  matrix products  69.2 us (11%)
  between operations  15.3 us (2%)
    unnamed x92, local copies, waits for them, and re-layouts  111 us
    ppermute x4, waiting for transfers between devices, reduce_to_first(): block = block + lax.ppermute(block, axis, pairs)  95.5 us
    ppermute x4, waiting for transfers between devices, broadcast_first(): got = lax.ppermute(block, axis, pairs)  78.6 us
    unnamed x6, other arithmetic  51.8 us
    dot_general x1, local copies, waits for them, and re-layouts, per_device(): jnp.dot(serve_hot.T, incoming.reshape(slot_total, -1), preferred_element_...  13.9 us
  transfers between devices with their start and end apart: 24, of which 7 were waited for; matrix products, arithmetic and copies ran while one was open for 44% of the time, Pallas kernels for 0%

commit v1 on v0

--- a/solution.py
+++ b/solution.py
@@ -6,6 +6,12 @@
 
 HEAD_SIZE = 128
 BLOCK_TOKENS = 64
+
+
+def bring_tracks_on_mesh(patch):
+    return jnp.concatenate(
+        lax.all_to_all(jnp.stack(jnp.split(patch, lax.psum(1, "head"), 2)), "head", 0, 0), axis=1
+    )
 
 
 def with_halo(block, sides, width):
@@ -51,7 +57,7 @@
     seq_count = lax.axis_size("seq")
     seq_index = lax.axis_index("seq")
     q_heads, k_heads, v_heads = (
-        lax.all_to_all(queries, "head", split_axis=2, concat_axis=1, tiled=True),
+        bring_tracks_on_mesh(queries),
         lax.all_to_all(key_rows, "head", split_axis=2, concat_axis=1, tiled=True),
         lax.all_to_all(values, "head", split_axis=2, concat_axis=1, tiled=True),
     )

time: 657 us -> 636 us (0.968)
  other arithmetic: 95.2 us -> 78.9 us
  waiting for transfers between devices: 175 us -> 187 us
  local copies, waits for them, and re-layouts: 209 us -> 200 us
    unnamed x92 -> x83, local copies, waits for them, and re-layouts: 111 us -> 94.5 us
    ppermute x4, waiting for transfers between devices: 78.6 us -> 94.2 us  [broadcast_first(): got = lax.ppermute(block, axis, pairs)]
    unnamed x6 -> x5, other arithmetic: 51.8 us -> 41.2 us
    all_to_all x3 -> x0, local copies, waits for them, and re-layouts: 10.5 us -> none  [per_device(): lax.all_to_all(queries, 'head', split_axis=2, concat_axis=1, tiled=True)]
    reshape x1, local copies, waits for them, and re-layouts: 1.81 us -> 10.4 us  [per_device(): grad_piece.reshape(block_count, block_len, head_count, head_dim)]
  transfers between devices with their start and end apart: 24 -> 24, of which waited for: 7 -> 7; matrix products, arithmetic and copies ran while one was open for 44% -> 43% of each run, Pallas kernels for 0% -> 0%
where the time goes in v1:
time: 636 us; the launch traced here: 625 us
  local copies, waits for them, and re-layouts  200 us (31%)
  waiting for transfers between devices  187 us (29%)
  starting transfers between devices  79.7 us (13%)
  other arithmetic  78.9 us (12%)
  matrix products  63.1 us (10%)
  between operations  15.3 us (2%)
    unnamed x83, local copies, waits for them, and re-layouts  94.5 us
    ppermute x4, waiting for transfers between devices, broadcast_first(): got = lax.ppermute(block, axis, pairs)  94.2 us
    ppermute x4, waiting for transfers between devices, reduce_to_first(): block = block + lax.ppermute(block, axis, pairs)  90.3 us
    unnamed x5, other arithmetic  41.2 us
    dot_general x1, local copies, waits for them, and re-layouts, per_device(): jnp.dot(serve_hot.T, incoming.reshape(slot_total, -1), preferred_element_...  14 us
  transfers between devices with their start and end apart: 24, of which 7 were waited for; matrix products, arithmetic and copies ran while one was open for 43% of the time, Pallas kernels for 0%

profile of v1, /device:TPU:0, one launch (start us, length us, event | category | flops | bytes accessed | tf_op | source)
XLA Modules:
  0.0 624.5 jit_solution(16771357670545297850)
XLA Ops:
  7.2 6.0 copy.153
  13.8 12.7 %reduce.18 = bf16[2048,160]{1,0:T(8,128)(2,1)S(1)} reduce(bf16[2048,1,160]{2,1,0:T(2,128)(2,1)} %bitcast.269, bf16[]{:T(256)} %broadcast.350), dimensions={1}, to_apply=%bitcast.224.reduce_sub_computation | reduce | bytes 1310722
  26.5 2.3 reshape.595
  28.8 4.6 all-to-all-start
  35.4 5.9 copy.156
  41.2 12.7 %reduce.19 = bf16[2048,160]{1,0:T(8,128)(2,1)S(1)} reduce(bf16[2048,1,160]{2,1,0:T(2,128)(2,1)} %bitcast.272, bf16[]{:T(256)} %broadcast.350), dimensions={1}, to_apply=%bitcast.222.reduce_sub_computation | reduce | bytes 1310722
  53.9 2.3 reshape.593
  56.3 4.8 all-to-all-start.1
  63.0 4.2 reshape.596
  67.2 4.5 copy.154
  72.3 7.9 %all-to-all-start.3 = ((s32[16,1,15]{2,1,0:T(1,128)}), s32[16,1,15]{2,1,0:T(1,128)S(1)}, u32[]{:S(2)}, u32[]{:S(2)}) async-start(s32[16,1,15]{2,1,0:T(1,128)} %bitcast.22), calls=%async_computation.3 | async-start | bytes 16384 | tf_op jit(solution)/shard_map/all_to_all | solution.py:88
  80.2 4.2 reshape.594
  84.4 5.7 copy.157
  93.2 4.1 collective-permute-start
  99.6 4.8 all-to-all-start.2
  106.3 4.7 pad_maximum_fusion.5
  112.8 3.7 copy.398
  116.6 3.4 reshape.544
  119.9 5.3 convolution_convert_fusion.1
  125.3 8.7 %copy.260 = bf16[30,8,64,256]{3,2,1,0:T(8,128)(2,1)} copy(bf16[30,8,64,256]{3,1,2,0:T(8,128)(2,1)} %bitcast.249) | data formatting | bytes 15728640
  134.0 8.2 %all-to-all-start.4 = ((bf16[16,15,64,256]{3,2,1,0:T(8,128)(2,1)}), bf16[16,15,64,256]{3,2,1,0:T(8,128)(2,1)}, u32[]{:S(2)}, u32[]{:S(2)}) async-start(bf16[16,15,64,256]{3,2,1,0:T(8,128)(2,1)} %bitcast.252), calls=%async_computation.4 | async-start | bytes 15728640 | tf_op jit(solution)/shard_map/all_to_all | solution.py:103
  143.3 3.8 collective-permute-start.2
  148.7 3.8 stack.46
  152.5 93.9 %collective-permute-done.2 = bf16[64,1024]{1,0:T(8,128)(2,1)S(1)} collective-permute-done((bf16[64,1024]{1,0:T(8,128)(2,1)S(1)}, bf16[64,1024]{1,0:T(8,128)(2,1)S(1)}, u32[]{:S(2)}, u32[]{:S(2)}) %collective-permute-start.2) | collective-permute-done | bytes 131104 | tf_op jit(solution)/shard_map/ppermute | solution.py:36
  247.8 3.8 stack.45
  251.5 3.8 stack.47
  255.3 4.9 pad_maximum_fusion.1
  266.5 2.9 select_reduce_fusion
  271.9 4.1 fusion.70
  276.1 10.4 %reshape.549 = bf16[10,64,4,128]{3,2,1,0:T(4,128)(2,1)S(1)} reshape(bf16[640,512]{1,0:T(8,128)(2,1)} %fusion.70) | data formatting | bytes 1310720 | tf_op jit(solution)/shard_map/reshape | solution.py:184
  286.5 14.4 %copy.261 = bf16[30,8,64,256]{3,1,2,0:T(8,128)(2,1)} copy(bf16[30,8,64,256]{3,2,1,0:T(8,128)(2,1)} %bitcast.110) | data formatting | bytes 15728640
  300.9 4.8 convolution_convert_fusion.2
  320.8 2.4 copy.233
  326.6 3.9 fusion.20
  331.0 2.6 fusion.101
  339.0 3.8 fusion.89
  342.8 3.7 pad_maximum_fusion
  347.4 3.7 copy.264
  353.4 5.7 copy.265
  359.1 8.7 %all-to-all-start.6 = ((bf16[16,15,64,256]{3,2,1,0:T(8,128)(2,1)}), bf16[16,15,64,256]{3,2,1,0:T(8,128)(2,1)}, u32[]{:S(2)}, u32[]{:S(2)}) async-start(bf16[16,15,64,256]{3,2,1,0:T(8,128)(2,1)} %bitcast.251), calls=%async_computation.7 | async-start | bytes 15728640 | tf_op jit(solution)/shard_map/all_to_all | solution.py:287
  371.6 4.7 multiply_convert_fusion.2
  381.1 3.3 copy_dynamic-update-slice_fusion.1
  384.4 4.0 copy_dynamic-update-slice_fusion
  390.6 57.8 %collective-permute-done.6 = f32[64,1024]{1,0:T(8,128)S(1)} collective-permute-done((f32[64,1024]{1,0:T(8,128)}, f32[64,1024]{1,0:T(8,128)S(1)}, u32[]{:S(2)}, u32[]{:S(2)}) %collective-permute-start.6) | collective-permute-done | bytes 262176 | tf_op jit(solution)/shard_map/ppermute | solution.py:49
  452.0 14.3 %collective-permute-done.7 = f32[64,1024]{1,0:T(8,128)S(1)} collective-permute-done((f32[64,1024]{1,0:T(8,128)S(1)}, f32[64,1024]{1,0:T(8,128)S(1)}, u32[]{:S(2)}, u32[]{:S(2)}) %collective-permute-start.7) | collective-permute-done | bytes 262176 | tf_op jit(solution)/shard_map/ppermute | solution.py:49
  469.8 10.6 %collective-permute-done.8 = f32[64,1024]{1,0:T(8,128)S(1)} collective-permute-done((f32[64,1024]{1,0:T(8,128)S(1)}, f32[64,1024]{1,0:T(8,128)S(1)}, u32[]{:S(2)}, u32[]{:S(2)}) %collective-permute-start.8) | collective-permute-done | bytes 262176 | tf_op jit(solution)/shard_map/ppermute | solution.py:49
  483.6 7.7 %collective-permute-done.9 = f32[64,1024]{1,0:T(8,128)S(1)} collective-permute-done((f32[64,1024]{1,0:T(8,128)S(1)}, f32[64,1024]{1,0:T(8,128)S(1)}, u32[]{:S(2)}, u32[]{:S(2)}) %collective-permute-start.9) | collective-permute-done | bytes 262176 | tf_op jit(solution)/shard_map/ppermute | solution.py:49
  496.1 5.2 collective-permute-start.10
  501.3 3.8 fusion.67
  506.4 4.9 broadcast_in_dim_reshape.6
  511.3 6.5 %reduce.20 = bf16[640,512]{1,0:T(8,128)(2,1)} reduce(bf16[640,1,512]{2,1,0:T(2,128)(2,1)} %bitcast.281, bf16[]{:T(256)} %broadcast.350), dimensions={1}, to_apply=%bitcast.226.reduce_sub_computation | reduce | bytes 1310722
  517.7 3.0 reshape.597
  523.8 2.9 reshape.553
  530.1 4.5 all-to-all-start.5
  534.5 14.9 %copy.266 = bf16[30,8,64,256]{3,1,2,0:T(8,128)(2,1)} copy(bf16[30,8,64,256]{3,2,1,0:T(8,128)(2,1)} %bitcast.125) | data formatting | bytes 15728640
  549.5 14.0 %dot_general.103 = bf16[64,2,128,240]{2,1,0,3:T(2,128)(2,1)} reshape(bf16[16384,240]{0,1:T(8,128)(2,1)} %bitcast.253) | data formatting | bytes 15728640 | tf_op jit(solution)/shard_map/dot_general | solution.py:288
  563.5 9.4 %fusion.6 = bf16[10,64,2,4,128]{4,0,2,1,3:T(8,128)(2,1)S(1)} fusion(f32[10,64,2,4,128]{4,3,2,1,0:T(4,128)S(1)} %copy-done.19, bf16[64,2,128,240]{2,1,0,3:T(2,128)(2,1)} %dot_general.103, s32[10,4]{0,1:T(4,128)S(1)} %multiply_add_fusion, s32[240]{0:T(256)S(1)} %eq.85), kind=kOutput, calls=%fused_computation.16 | convolution fusion | flops 315893120 | bytes 11797600 | tf_op jit(solution)/shard_map/dot_general | solution.py:288
  574.1 4.7 reduce.22
  580.1 5.4 all-to-all-start.8
  585.6 2.3 reshape.598
  590.3 3.7 convert_element_type.110
  594.0 4.7 reduce.21
  600.0 4.8 all-to-all-start.7
  604.8 5.0 broadcast_multiply_fusion
  (214 shorter events, 101.7 us)
Async XLA Ops:
  7.2 264.8 %copy-start = (bf16[512,2048]{1,0:T(8,128)(2,1)S(1)}, bf16[512,2048]{1,0:T(8,128)(2,1)}, u32[]{:S(2)}) copy-start(bf16[512,2048]{1,0:T(8,128)(2,1)} %param.22) | copy-start | bytes 6291460
  13.8 19.6 %copy-start.27 = (s32[10,4,4]{0,2,1:T(4,128)S(1)}, s32[10,4,4]{0,2,1:T(4,128)}, u32[]{:S(2)}) copy-start(s32[10,4,4]{0,2,1:T(4,128)} %param.21) | copy-start | bytes 1924
  28.8 27.4 %all-to-all-start = ((bf16[4,2,40960]{2,1,0:T(2,128)(2,1)}), bf16[4,2,40960]{2,1,0:T(2,128)(2,1)}, u32[]{:S(2)}, u32[]{:S(2)}) async-start(bf16[4,2,40960]{2,1,0:T(2,128)(2,1)} %reshape.595), calls=%async_computation | async-start | bytes 1310720 | tf_op jit(solution)/shard_map/all_to_all | solution.py:61
  56.3 16.0 %all-to-all-start.1 = ((bf16[4,2,40960]{2,1,0:T(2,128)(2,1)}), bf16[4,2,40960]{2,1,0:T(2,128)(2,1)}, u32[]{:S(2)}, u32[]{:S(2)}) async-start(bf16[4,2,40960]{2,1,0:T(2,128)(2,1)} %reshape.593), calls=%async_computation.1 | async-start | bytes 1310720 | tf_op jit(solution)/shard_map/all_to_all | solution.py:62
  61.2 6.0 copy-start.28
  72.3 20.1 %copy-start.15 = (bf16[1,4,160,512]{3,2,1,0:T(8,128)(2,1)}, bf16[1,4,160,512]{3,2,1,0:T(8,128)(2,1)S(1)}, u32[]{:S(2)}) copy-start(bf16[1,4,160,512]{3,2,1,0:T(8,128)(2,1)S(1)} %copy.155) | copy-start | bytes 1966084
  72.3 27.3 %all-to-all-start.3 = ((s32[16,1,15]{2,1,0:T(1,128)}), s32[16,1,15]{2,1,0:T(1,128)S(1)}, u32[]{:S(2)}, u32[]{:S(2)}) async-start(s32[16,1,15]{2,1,0:T(1,128)} %bitcast.22), calls=%async_computation.3 | async-start | bytes 16384 | tf_op jit(solution)/shard_map/all_to_all | solution.py:88
  92.2 6.4 %copy-start.23 = (bf16[1,160,2048]{2,1,0:T(8,128)(2,1)S(1)}, bf16[1,160,2048]{2,1,0:T(8,128)(2,1)}, u32[]{:S(2)}) copy-start(bf16[1,160,2048]{2,1,0:T(8,128)(2,1)} %param.18) | copy-start | bytes 1966084
  92.3 0.8 copy-start.16
  93.2 12.5 %collective-permute-start = (bf16[64,1024]{1,0:T(8,128)(2,1)S(1)}, bf16[64,1024]{1,0:T(8,128)(2,1)S(1)}, u32[]{:S(2)}, u32[]{:S(2)}) collective-permute-start(bf16[64,1024]{1,0:T(8,128)(2,1)S(1)} %get-tuple-element.96), channel_id=1, source_target_pairs={{0,4},{4,8},{8,12},{12,16},{16,20},{20,24},{24,28},{28,32},{32,36}... | collective-permute-start | bytes 393224 | tf_op jit(solution)/shard_map/ppermute | solution.py:22
  97.3 9.0 %collective-permute-start.1 = (bf16[64,1024]{1,0:T(8,128)(2,1)S(1)}, bf16[64,1024]{1,0:T(8,128)(2,1)}, u32[]{:S(2)}, u32[]{:S(2)}) collective-permute-start(bf16[64,1024]{1,0:T(8,128)(2,1)S(1)} %get-tuple-element.97), channel_id=1, source_target_pairs={{4,0},{8,4},{12,8},{16,12},{20,16},{24,20},{28,24},{32,28},{36,32}... | collective-permute-start | bytes 393224 | tf_op jit(solution)/shard_map/ppermute | solution.py:25
  99.6 34.4 %all-to-all-start.2 = ((bf16[4,1,160,512]{3,2,1,0:T(8,128)(2,1)}), bf16[4,1,160,512]{3,2,1,0:T(8,128)(2,1)}, u32[]{:S(2)}, u32[]{:S(2)}) async-start(bf16[4,1,160,512]{3,2,1,0:T(8,128)(2,1)} %pad_maximum_fusion.7), calls=%async_computation.2 | async-start | bytes 1310720 | tf_op jit(solution)/shard_map/all_to_all | solution.py:13
  105.7 0.7 copy-start.26
  111.0 5.6 copy-start.9
  134.0 13.1 %copy-start.29 = (s32[160]{0:T(256)S(1)}, s32[160]{0:T(256)}, u32[]{:S(2)}) copy-start(s32[160]{0:T(256)} %copy-done.28) | copy-start | bytes 1924
  134.0 152.5 %all-to-all-start.4 = ((bf16[16,15,64,256]{3,2,1,0:T(8,128)(2,1)}), bf16[16,15,64,256]{3,2,1,0:T(8,128)(2,1)}, u32[]{:S(2)}, u32[]{:S(2)}) async-start(bf16[16,15,64,256]{3,2,1,0:T(8,128)(2,1)} %bitcast.252), calls=%async_computation.4 | async-start | bytes 15728640 | tf_op jit(solution)/shard_map/all_to_all | solution.py:103
  142.2 129.8 %all-gather.2.cloned.1.call-start = ((), (), s32[]{:S(2)}) async-start(), calls=%async_computation.11 | async-start | bytes 3276800 | tf_op jit(solution)/shard_map/all_gather | solution.py:177
  142.9 461.9 %all-reduce.4.cloned.1.call-start = ((), (), s32[]{:S(2)}) async-start(), calls=%async_computation.12 | async-start | bytes 8388608 | tf_op jit(solution)/shard_map/psum | solution.py:183
  143.3 103.2 %collective-permute-start.2 = (bf16[64,1024]{1,0:T(8,128)(2,1)S(1)}, bf16[64,1024]{1,0:T(8,128)(2,1)S(1)}, u32[]{:S(2)}, u32[]{:S(2)}) collective-permute-start(bf16[64,1024]{1,0:T(8,128)(2,1)S(1)} %get-tuple-element.97), channel_id=1, source_target_pairs={{0,4},{1,5},{2,6},{3,7},{64,68},{65,69},{66,70},{67,71}} | collective-permute-start | bytes 393224 | tf_op jit(solution)/shard_map/ppermute | solution.py:36
  246.5 14.8 %collective-permute-start.3 = (bf16[64,1024]{1,0:T(8,128)(2,1)S(1)}, bf16[64,1024]{1,0:T(8,128)(2,1)S(1)}, u32[]{:S(2)}, u32[]{:S(2)}) collective-permute-start(bf16[64,1024]{1,0:T(8,128)(2,1)S(1)} %broadcast_select_fusion), channel_id=1, source_target_pairs={{0,8},{4,12},{1,9},{5,13},{2,10},{6,14},{3,11},{7,15},{64,72},{68,... | collective-permute-start | bytes 393224 | tf_op jit(solution)/shard_map/ppermute | solution.py:36
  261.3 5.2 copy-start.8
  261.3 3.8 collective-permute-start.4
  265.1 4.2 collective-permute-start.5
  309.1 1.5 copy-start.2
  309.1 2.3 copy-start.6
  309.1 3.1 copy-start.10
  313.2 1.5 copy-start.24
  315.1 1.5 copy-start.22
  320.8 2.4 copy-start.4
  323.2 3.4 copy-start.18
  325.8 0.8 copy-start.13
  330.5 284.8 %reduce-scatter.2.cloned.1.call-start = ((), (), s32[]{:S(2)}) async-start(), calls=%async_computation.10 | async-start | bytes 6553600 | tf_op jit(solution)/shard_map/reduce_scatter | solution.py:171
  333.6 2.2 copy-start.12
  336.6 2.3 copy-start.14
  359.1 8.7 %copy-start.7 = (f32[4,10,64,64]{2,3,1,0:T(8,128)S(1)}, f32[4,10,64,64]{2,3,1,0:T(8,128)}, u32[]{:S(2)}) copy-start(f32[4,10,64,64]{2,3,1,0:T(8,128)} %get-tuple-element.117) | copy-start | bytes 1966084
  359.1 8.7 %copy-start.25 = (bf16[64,1,4,128]{3,2,1,0:T(4,128)(2,1)S(1)}, bf16[64,1,4,128]{3,2,1,0:T(4,128)(2,1)}, u32[]{:S(2)}) copy-start(bf16[64,1,4,128]{3,2,1,0:T(4,128)(2,1)} %get-tuple-element.102) | copy-start | bytes 196612
  359.1 171.0 %all-to-all-start.6 = ((bf16[16,15,64,256]{3,2,1,0:T(8,128)(2,1)}), bf16[16,15,64,256]{3,2,1,0:T(8,128)(2,1)}, u32[]{:S(2)}, u32[]{:S(2)}) async-start(bf16[16,15,64,256]{3,2,1,0:T(8,128)(2,1)} %bitcast.251), calls=%async_computation.7 | async-start | bytes 15728640 | tf_op jit(solution)/shard_map/all_to_all | solution.py:287
  368.5 1.7 copy-start.20
  370.3 78.0 %collective-permute-start.6 = (f32[64,1024]{1,0:T(8,128)}, f32[64,1024]{1,0:T(8,128)S(1)}, u32[]{:S(2)}, u32[]{:S(2)}) collective-permute-start(f32[64,1024]{1,0:T(8,128)} %reshape.552), channel_id=1, source_target_pairs={{32,0},{36,4},{40,8},{44,12},{48,16},{52,20},{56,24},{60,28},{33,1... | collective-permute-start | bytes 786440 | tf_op jit(solution)/shard_map/ppermute | solution.py:49
  376.3 1.1 copy-start.17
  377.4 1.7 copy-start.11
  449.3 18.4 %copy-start.3 = (bf16[10,4,4,64,128]{4,3,2,1,0:T(8,128)(2,1)S(1)}, bf16[10,4,4,64,128]{4,3,2,1,0:T(8,128)(2,1)}, u32[]{:S(2)}) copy-start(bf16[10,4,4,64,128]{4,3,2,1,0:T(8,128)(2,1)} %copy-done.2) | copy-start | bytes 7864324
  449.3 18.4 %copy-start.5 = (bf16[4,10,64,4,64]{2,4,3,1,0:T(8,128)(2,1)S(1)}, bf16[4,10,64,4,64]{2,4,3,1,0:T(8,128)(2,1)}, u32[]{:S(2)}) copy-start(bf16[4,10,64,4,64]{2,4,3,1,0:T(8,128)(2,1)} %copy-done.4) | copy-start | bytes 3932164
  449.3 16.9 %collective-permute-start.7 = (f32[64,1024]{1,0:T(8,128)S(1)}, f32[64,1024]{1,0:T(8,128)S(1)}, u32[]{:S(2)}, u32[]{:S(2)}) collective-permute-start(f32[64,1024]{1,0:T(8,128)S(1)} %add.228), channel_id=1, source_target_pairs={{16,0},{20,4},{24,8},{28,12},{17,1},{21,5},{25,9},{29,13},{18,2},{... | collective-permute-start | bytes 786440 | tf_op jit(solution)/shard_map/ppermute | solution.py:49
  466.3 15.9 %copy-start.21 = (bf16[4,10,64,64]{2,3,1,0:T(8,128)(2,1)S(1)}, bf16[4,10,64,64]{2,3,1,0:T(8,128)(2,1)}, u32[]{:S(2)}) copy-start(bf16[4,10,64,64]{2,3,1,0:T(8,128)(2,1)} %copy-done.20) | copy-start | bytes 983044
  466.3 14.1 %collective-permute-start.8 = (f32[64,1024]{1,0:T(8,128)S(1)}, f32[64,1024]{1,0:T(8,128)S(1)}, u32[]{:S(2)}, u32[]{:S(2)}) collective-permute-start(f32[64,1024]{1,0:T(8,128)S(1)} %add.229), channel_id=1, source_target_pairs={{8,0},{12,4},{9,1},{13,5},{10,2},{14,6},{11,3},{15,7},{72,64},{76,... | collective-permute-start | bytes 786440 | tf_op jit(solution)/shard_map/ppermute | solution.py:49
  480.4 10.8 %collective-permute-start.9 = (f32[64,1024]{1,0:T(8,128)S(1)}, f32[64,1024]{1,0:T(8,128)S(1)}, u32[]{:S(2)}, u32[]{:S(2)}) collective-permute-start(f32[64,1024]{1,0:T(8,128)S(1)} %add.230), channel_id=1, source_target_pairs={{4,0},{5,1},{6,2},{7,3},{68,64},{69,65},{70,66},{71,67}} | collective-permute-start | bytes 786440 | tf_op jit(solution)/shard_map/ppermute | solution.py:49
  494.8 31.9 %collective-permute-start.11 = (bf16[64,1024]{1,0:T(8,128)(2,1)S(1)}, bf16[64,1024]{1,0:T(8,128)(2,1)S(1)}, u32[]{:S(2)}, u32[]{:S(2)}) collective-permute-start(bf16[64,1024]{1,0:T(8,128)(2,1)S(1)} %concatenate.41), channel_id=1, source_target_pairs={{4,0},{8,4},{12,8},{16,12},{20,16},{24,20},{28,24},{32,28},{36,32}... | collective-permute-start | bytes 393224 | tf_op jit(solution)/shard_map/ppermute | solution.py:25
  496.1 30.6 %collective-permute-start.10 = (bf16[64,1024]{1,0:T(8,128)(2,1)S(1)}, bf16[64,1024]{1,0:T(8,128)(2,1)}, u32[]{:S(2)}, u32[]{:S(2)}) collective-permute-start(bf16[64,1024]{1,0:T(8,128)(2,1)S(1)} %concatenate.40), channel_id=1, source_target_pairs={{0,4},{4,8},{8,12},{12,16},{16,20},{20,24},{24,28},{28,32},{32,36}... | collective-permute-start | bytes 393224 | tf_op jit(solution)/shard_map/ppermute | solution.py:22
  530.1 50.0 %all-to-all-start.5 = ((bf16[4,2,40960]{2,1,0:T(2,128)(2,1)}), bf16[4,2,40960]{2,1,0:T(2,128)(2,1)}, u32[]{:S(2)}, u32[]{:S(2)}) async-start(bf16[4,2,40960]{2,1,0:T(2,128)(2,1)} %reshape.597), calls=%async_computation.6 | async-start | bytes 1310720 | tf_op jit(solution)/shard_map/all_to_all | solution.py:296
  549.5 14.0 %copy-start.19 = (f32[10,64,2,4,128]{4,3,2,1,0:T(4,128)S(1)}, f32[10,64,2,4,128]{4,3,2,1,0:T(4,128)}, u32[]{:S(2)}) copy-start(f32[10,64,2,4,128]{4,3,2,1,0:T(4,128)} %reshape.555) | copy-start | bytes 7864324
  580.1 19.9 %all-to-all-start.8 = ((bf16[4,2,40960]{2,1,0:T(2,128)(2,1)}), bf16[4,2,40960]{2,1,0:T(2,128)(2,1)S(1)}, u32[]{:S(2)}, u32[]{:S(2)}) async-start(bf16[4,2,40960]{2,1,0:T(2,128)(2,1)} %reshape.601), calls=%async_computation.9 | async-start | bytes 1310720 | tf_op jit(solution)/shard_map/all_to_all | solution.py:298
  600.0 13.6 %all-to-all-start.7 = ((bf16[4,2,40960]{2,1,0:T(2,128)(2,1)}), bf16[4,2,40960]{2,1,0:T(2,128)(2,1)S(1)}, u32[]{:S(2)}, u32[]{:S(2)}) async-start(bf16[4,2,40960]{2,1,0:T(2,128)(2,1)} %reshape.599), calls=%async_computation.8 | async-start | bytes 1310720 | tf_op jit(solution)/shard_map/all_to_all | solution.py:297
  614.2 3.3 copy-start.1
Sparse Core Ops, SparseCore 0:
  144.6 37.1 all-gather.1
  330.7 195.9 all-reduce.3
  529.0 58.2 reduce-scatter.1
